TPU v7x, 512 devices: a whole 4x8x8 slice. The times are simulated.
512 devices in a mesh: fsdp: 128 (over y, z, core), tensor: 4 (over x).
Axes of the slice: x: 4, y: 8, z: 8, core: 2. Of those that a mesh axis runs over, the one named last changes fastest.
Arguments:
- layer_inputs: bfloat16 [2, 49152, 5120], P(None, 'fsdp', 'tensor'), may hold values from -8 to 8, as said below
- out_grads: bfloat16 [2, 49152, 2560], P(None, 'fsdp', 'tensor'), may hold values from -8 to 8, as said below
- weight_grad: bfloat16 [2, 2560, 5120], P(None, 'fsdp', 'tensor'), may hold values from -0.059814453 to 0.059814453
- emb_grad: bfloat16 [50176, 2560], P('fsdp', 'tensor'), may hold values from -0.59765625 to 0.59765625
- counts: int32 [50176], P('fsdp'), may hold values from 0 to 250
- owner_pos: int32 [4, 30], P('tensor'), may hold values from 0 to 127, as said below
Outputs:
- update: bfloat16 [2, 2560, 5120], P(None, 'fsdp', 'tensor')
- owner_inverses: float32 [4, 128, 128, 128], P('tensor', 'fsdp')
- emb_update: bfloat16 [50176, 2560], P('fsdp', 'tensor')
Inputs may be any that keep to these rules, and one draw needn't show every extreme that they name: `layer_inputs`: every element lies within the stated range; inner units in groups of four share a common part. `out_grads`: every element lies within the stated range; features in groups of four share a common part. `owner_pos`: the 30 entries of a row are distinct; slot p belongs to fsdp index p; some fsdp index holds 1 block of each row.
All inputs are finite; a program needn't handle non-finite values. Where the computation divides by a largest or mean magnitude, that divisor is 1e-20 or more.
Results may differ from a plain program's by a relative error of at most 0.0062.
Values may be sent and summed in bfloat16 or wider, within the bound.
No kernel may reach another device: no remote copies, remote signals or barrier semaphores. Data moves between devices by JAX's collectives and lax.ppermute only.
A program may use at most 64 MiB of HBM per device.

v0:
```python
import jax
import jax.numpy as jnp
from jax import lax
from jax.sharding import PartitionSpec as P

BLK = 128
NS_ITERS = 8
DAMP = 0.02
EDAMP = 0.25


def newton_inverse(factor):
    identity = jnp.eye(factor.shape[-1], dtype=jnp.float32)
    damped = factor + DAMP * identity
    norm_scale = jnp.max(jnp.sum(jnp.abs(damped), axis=-1), axis=-1)
    approx = identity[None] / norm_scale[:, None, None]
    for sweep_idx in range(NS_ITERS):
        product = jnp.einsum("bij,bjk->bik", damped, approx, precision=lax.Precision.HIGHEST)
        approx = jnp.einsum(
            "bij,bjk->bik", approx, 2.0 * identity[None] - product, precision=lax.Precision.HIGHEST
        )
    return approx


def on_device(layer_inputs, out_grads, weight_grad, emb_grad, counts, owner_pos):
    fsdp_size = lax.axis_size("fsdp")
    layers, row_count, inner_local = layer_inputs.shape
    width_local = out_grads.shape[2]
    a_count = inner_local // BLK
    g_count = width_local // BLK
    input_blocks = layer_inputs.reshape(layers, row_count, a_count, BLK)
    a_part = jnp.einsum(
        "lrbi,lrbj->lbij", input_blocks, input_blocks, preferred_element_type=jnp.float32
    )
    grad_blocks = out_grads.reshape(layers, row_count, g_count, BLK)
    g_part = jnp.einsum(
        "lrbi,lrbj->lbij", grad_blocks, grad_blocks, preferred_element_type=jnp.float32
    )
    partials = jnp.concatenate([a_part, g_part], axis=1)
    count_part = jnp.sum(counts.astype(jnp.float32))
    block_total = layers * (a_count + g_count)
    own_table = owner_pos[0]
    slot_count = (block_total + fsdp_size - 1) // fsdp_size
    wanted = lax.axis_index("fsdp") * slot_count + jnp.arange(slot_count, dtype=jnp.int32)
    one_hot = (own_table[None, :] == wanted[:, None]).astype(jnp.float32)
    divisor = row_count * fsdp_size
    summed, count_total = lax.psum((partials, count_part), "fsdp")
    factors = (summed / divisor).reshape(-1, BLK, BLK)
    mine_blocks = jnp.einsum("sk,kij->sij", one_hot, factors, precision=lax.Precision.HIGHEST)
    held_inv = newton_inverse(mine_blocks) * jnp.max(one_hot, axis=1)[:, None, None]
    owner_out = held_inv[None]
    shared = lax.all_gather(held_inv.astype(jnp.bfloat16), "fsdp", axis=0, tiled=True)
    low_inv = jnp.take(shared, own_table, axis=0)
    low_inv = low_inv.reshape(layers, a_count + g_count, BLK, BLK)
    a_low = low_inv[:, :a_count]
    g_own = low_inv[:, a_count:]
    g_all = lax.all_gather(g_own, "tensor", axis=1, tiled=True)
    d_local = weight_grad.shape[1]
    grad_split = weight_grad.reshape(layers, d_local, a_count, BLK)
    right_done = jnp.einsum(
        "ldbi,lbij->ldbj", grad_split, a_low, preferred_element_type=jnp.float32
    )
    right_done = right_done.reshape(layers, d_local, inner_local).astype(jnp.bfloat16)
    columns = lax.all_to_all(right_done, "fsdp", split_axis=2, concat_axis=1, tiled=True)
    full_width = columns.shape[1]
    column_blocks = columns.reshape(layers, full_width // BLK, BLK, columns.shape[2])
    left_done = jnp.einsum(
        "lbij,lbjc->lbic", g_all, column_blocks, preferred_element_type=jnp.float32
    )
    left_done = left_done.reshape(columns.shape).astype(jnp.bfloat16)
    update = lax.all_to_all(left_done, "fsdp", split_axis=1, concat_axis=2, tiled=True)
    vocab_total = counts.shape[0] * fsdp_size
    frequency = counts.astype(jnp.float32) * vocab_total / count_total
    emb_update = (emb_grad.astype(jnp.float32) / (frequency + EDAMP)[:, None]).astype(jnp.bfloat16)
    return (update, owner_out, emb_update)


def solution(mesh):
    placed = (
        P(None, "fsdp", "tensor"),
        P(None, "fsdp", "tensor"),
        P(None, "fsdp", "tensor"),
        P("fsdp", "tensor"),
        P("fsdp"),
        P("tensor", None),
    )
    return jax.shard_map(
        on_device,
        mesh=mesh,
        in_specs=placed,
        out_specs=(P(None, "fsdp", "tensor"), P("tensor", "fsdp", None, None), P("fsdp", "tensor")),
        check_vma=False,
    )
```

profile of v0, /device:TPU:1, one launch (start us, length us, event | category | flops | bytes accessed | tf_op | source)
XLA Modules:
  0.0 627.3 jit_solution(3849056643370400006)
XLA Ops:
  7.2 2.8 copy.41
  10.1 0.9 fusion.20
  11.0 1.6 copy.43
  12.6 0.5 fusion.21
  13.1 1.4 pad_maximum_fusion
  14.6 0.6 copy-done.3
  15.2 0.6 fusion.14
  15.8 206.1 %all-reduce.2.cloned.1.call-done = f32[2,15,128,128]{3,2,1,0:T(8,128)} async-done(((f32[2,15,128,128]{3,2,1,0:T(8,128)}), f32[2,15,128,128]{3,2,1,0:T(8,128)}) %all-reduce.2.cloned.1.call-update) | async-done | bytes 1966096 | tf_op jit(solution)/shard_map/psum | solution.py:47
  221.9 1.7 broadcast_multiply_fusion
  223.6 1.9 fusion
  225.6 0.6 reduce_max.18
  226.9 0.2 convolution_subtract_fusion.7
  227.1 0.2 fusion.5
  227.3 0.2 convolution_subtract_fusion.6
  227.8 0.2 convolution_subtract_fusion.5
  228.0 0.2 fusion.23
  228.2 0.2 convolution_subtract_fusion.4
  228.6 0.2 convolution_subtract_fusion.3
  229.0 0.2 convolution_subtract_fusion.2
  229.2 0.2 fusion.26
  229.5 0.2 convolution_subtract_fusion.1
  229.9 0.2 convolution_subtract_fusion
  230.1 1.5 fusion.19
  231.7 0.5 broadcast.106
  232.2 0.7 reduce.8
  232.9 81.3 %all-gather.6.cloned.1.call-done = bf16[16384,128]{1,0:T(8,128)(2,1)} async-done(((bf16[128,128]{1,0:T(8,128)(2,1)}), bf16[16384,128]{1,0:T(8,128)(2,1)}) %all-gather.6.cloned.1.call-update) | async-done | bytes 4194320 | tf_op jit(solution)/shard_map/all_gather | solution.py:52
  314.3 2.9 gather_fusion
  317.4 0.7 slice.10
  318.2 0.6 convert_reduce_fusion
  318.8 247.1 %psum.15 = f32[]{:T(128)} all-reduce(f32[]{:T(128)} %convert_reduce_fusion), channel_id=1, replica_groups=mesh['fsdp'=128,'tensor'=4] {'fsdp'}, use_global_device_ids=true, to_apply=%region_5.0 | all-reduce | flops 1 | bytes 8 | tf_op jit(solution)/shard_map/psum | solution.py:47
  565.9 0.3 fusion.2
  566.2 0.5 copy.59
  566.7 1.2 reshape.204
  567.9 10.2 %all-to-all-start = ((bf16[128,2,200]{2,1,0:T(2,128)(2,1)}), bf16[128,2,200]{2,1,0:T(2,128)(2,1)S(1)}, u32[]{:S(2)}, u32[]{:S(2)}) async-start(bf16[128,2,200]{2,1,0:T(2,128)(2,1)} %reshape.204), calls=%async_computation | async-start | bytes 262144 | tf_op jit(solution)/shard_map/all_to_all | solution.py:64
  578.1 0.7 divide_add_fusion
  578.7 11.6 %all-to-all-done = bf16[128,2,200]{2,1,0:T(2,128)(2,1)S(1)} async-done(((bf16[128,2,200]{2,1,0:T(2,128)(2,1)}), bf16[128,2,200]{2,1,0:T(2,128)(2,1)S(1)}, u32[]{:S(2)}, u32[]{:S(2)}) %all-to-all-start) | async-done | bytes 102432 | tf_op jit(solution)/shard_map/all_to_all | solution.py:64
  590.3 0.6 reshape.205
  591.1 1.4 reshape.183
  592.5 2.1 convolution_convert_fusion
  594.5 1.1 copy.60
  595.6 1.6 reshape.206
  597.2 6.1 all-to-all-start.1
  603.4 1.0 divide_convert_fusion
  604.3 11.4 %all-to-all-done.1 = bf16[128,2,200]{2,1,0:T(2,128)(2,1)S(1)} async-done(((bf16[128,2,200]{2,1,0:T(2,128)(2,1)}), bf16[128,2,200]{2,1,0:T(2,128)(2,1)S(1)}, u32[]{:S(2)}, u32[]{:S(2)}) %all-to-all-start.1) | async-done | bytes 102432 | tf_op jit(solution)/shard_map/all_to_all | solution.py:71
  615.7 1.0 reshape.207
  616.7 2.3 copy.61
  619.0 0.7 copy.53
  619.7 1.1 copy.54
  (26 shorter events, 1.6 us)
Async XLA Ops:
  7.2 214.7 %all-reduce.2.cloned.1.call-start = ((), (), s32[]{:S(2)}) async-start(), calls=%async_computation.2 | async-start | bytes 3932160 | tf_op jit(solution)/shard_map/psum | solution.py:47
  14.6 0.7 copy-start.3
  14.6 299.7 %all-gather.6.cloned.1.call-start = ((), (), s32[]{:S(2)}) async-start(), calls=%async_computation.4 | async-start | bytes 4227072 | tf_op jit(solution)/shard_map/all_gather | solution.py:52
  231.6 360.8 %all-gather.4.cloned.1.call-start = ((), (), s32[]{:S(2)}) async-start(), calls=%async_computation.3 | async-start | bytes 1638400 | tf_op jit(solution)/shard_map/all_gather | solution.py:57
  317.2 1.0 copy-start.2
  317.2 248.6 %copy-start.1 = (bf16[2,20,1280]{2,0,1:T(2,128)(2,1)S(1)}, bf16[2,20,1280]{2,0,1:T(2,128)(2,1)}, u32[]{:S(2)}) copy-start(bf16[2,20,1280]{2,0,1:T(2,128)(2,1)} %param.8) | copy-start | bytes 307204
  567.9 22.4 %all-to-all-start = ((bf16[128,2,200]{2,1,0:T(2,128)(2,1)}), bf16[128,2,200]{2,1,0:T(2,128)(2,1)S(1)}, u32[]{:S(2)}, u32[]{:S(2)}) async-start(bf16[128,2,200]{2,1,0:T(2,128)(2,1)} %reshape.204), calls=%async_computation | async-start | bytes 262144 | tf_op jit(solution)/shard_map/all_to_all | solution.py:64
  594.5 8.8 %copy-start = (bf16[392,640]{1,0:T(8,128)(2,1)S(1)}, bf16[392,640]{1,0:T(8,128)(2,1)}, u32[]{:S(2)}) copy-start(bf16[392,640]{1,0:T(8,128)(2,1)} %param.9) | copy-start | bytes 1505284
  597.2 18.5 %all-to-all-start.1 = ((bf16[128,2,200]{2,1,0:T(2,128)(2,1)}), bf16[128,2,200]{2,1,0:T(2,128)(2,1)S(1)}, u32[]{:S(2)}, u32[]{:S(2)}) async-start(bf16[128,2,200]{2,1,0:T(2,128)(2,1)} %reshape.206), calls=%async_computation.1 | async-start | bytes 262144 | tf_op jit(solution)/shard_map/all_to_all | solution.py:71
Sparse Core Ops, SparseCore 0:
  14.7 207.1 all-reduce.1
  231.7 82.4 all-gather.5
  318.3 25.3 all-gather.3
where the time goes:
time: 628 us; the launch traced here: 627 us
  waiting for transfers between devices  310 us (49%)
  blocking collectives  247 us (39%)
  local copies, waits for them, and re-layouts  20.9 us (3%)
  starting transfers between devices  16.4 us (3%)
  between operations  14.8 us (2%)
  matrix products  10.3 us (2%)
  other arithmetic  7.5 us (1%)
    psum x1, blocking collectives, on_device(): summed, count_total = lax.psum((partials, count_part), 'fsdp')  247 us
    psum x1, waiting for transfers between devices, on_device(): summed, count_total = lax.psum((partials, count_part), 'fsdp')  206 us
    all_gather x1, waiting for transfers between devices, on_device(): lax.all_gather(held_inv.astype(jnp.bfloat16), 'fsdp', axis=0, tiled=True)  81.3 us
  transfers between devices with their start and end apart: 5, of which 4 were waited for; matrix products, arithmetic and copies ran while one was open for 1% of the time, Pallas kernels for 0%

commit v1 on v0

--- a/solution.py
+++ b/solution.py
@@ -61,7 +61,9 @@
         "ldbi,lbij->ldbj", grad_split, a_low, preferred_element_type=jnp.float32
     )
     right_done = right_done.reshape(layers, d_local, inner_local).astype(jnp.bfloat16)
-    columns = lax.all_to_all(right_done, "fsdp", split_axis=2, concat_axis=1, tiled=True)
+    pieces = jnp.split(right_done, lax.axis_size("fsdp"), axis=2)
+    incoming = lax.all_to_all(jnp.stack(pieces), "fsdp", 0, 0)
+    columns = jnp.concatenate(incoming, axis=1)
     full_width = columns.shape[1]
     column_blocks = columns.reshape(layers, full_width // BLK, BLK, columns.shape[2])
     left_done = jnp.einsum(

time: 628 us -> 571 us (0.909)
  waiting for transfers between devices: 310 us -> 229 us
  local copies, waits for them, and re-layouts: 20.9 us -> 37.3 us
  starting transfers between devices: 16.4 us -> 23.3 us
    all_gather x1, waiting for transfers between devices: 81.3 us -> 0.02 us  [on_device(): lax.all_gather(held_inv.astype(jnp.bfloat16), 'fsdp', axis=0, tiled=True)]
    unnamed x16 -> x143, local copies, waits for them, and re-layouts: 11 us -> 22.3 us
    another operation x0 -> x3, local copies, waits for them, and re-layouts: none -> 6.48 us  [the longest x2 5.13 us: on_device(): incoming = lax.all_to_all(jnp.stack(pieces), 'fsdp', 0, 0)]
  transfers between devices with their start and end apart: 5 -> 5, of which waited for: 4 -> 3; matrix products, arithmetic and copies ran while one was open for 1% -> 2% of each run, Pallas kernels for 0% -> 0%
where the time goes in v1:
time: 571 us; the launch traced here: 570 us
  blocking collectives  248 us (43%)
  waiting for transfers between devices  229 us (40%)
  local copies, waits for them, and re-layouts  37.3 us (7%)
  starting transfers between devices  23.3 us (4%)
  between operations  15 us (3%)
  matrix products  10.3 us (2%)
  other arithmetic  7.53 us (1%)
    psum x1, blocking collectives, on_device(): summed, count_total = lax.psum((partials, count_part), 'fsdp')  248 us
    psum x1, waiting for transfers between devices, on_device(): summed, count_total = lax.psum((partials, count_part), 'fsdp')  206 us
    unnamed x143, local copies, waits for them, and re-layouts  22.3 us
    all_to_all x1, starting transfers between devices, on_device(): incoming = lax.all_to_all(jnp.stack(pieces), 'fsdp', 0, 0)  13.1 us
    all_to_all x1, waiting for transfers between devices, on_device(): incoming = lax.all_to_all(jnp.stack(pieces), 'fsdp', 0, 0)  11.6 us
  transfers between devices with their start and end apart: 5, of which 3 were waited for; matrix products, arithmetic and copies ran while one was open for 2% of the time, Pallas kernels for 0%

profile of v1, /device:TPU:1, one launch (start us, length us, event | category | flops | bytes accessed | tf_op | source)
XLA Modules:
  0.0 570.1 jit_solution(7782323773077567545)
XLA Ops:
  7.2 2.8 copy.309
  10.1 0.9 fusion.20
  11.0 1.6 copy.311
  12.6 0.5 fusion.21
  13.1 1.5 pad_maximum_fusion
  14.7 0.6 copy-done.3
  15.3 0.6 fusion.14
  15.9 206.1 %all-reduce.2.cloned.1.call-done = f32[2,15,128,128]{3,2,1,0:T(8,128)} async-done(((f32[2,15,128,128]{3,2,1,0:T(8,128)}), f32[2,15,128,128]{3,2,1,0:T(8,128)}) %all-reduce.2.cloned.1.call-update) | async-done | bytes 1966096 | tf_op jit(solution)/shard_map/psum | solution.py:47
  221.9 1.7 broadcast_multiply_fusion
  223.7 1.9 fusion
  225.7 0.6 reduce_max.18
  227.0 0.2 convolution_subtract_fusion.7
  227.4 0.2 convolution_subtract_fusion.6
  227.8 0.2 convolution_subtract_fusion.5
  228.1 0.2 fusion.23
  228.3 0.2 convolution_subtract_fusion.4
  228.5 0.2 fusion.24
  228.7 0.2 convolution_subtract_fusion.3
  229.1 0.2 convolution_subtract_fusion.2
  229.3 0.2 fusion.26
  229.5 0.2 convolution_subtract_fusion.1
  230.0 0.2 convolution_subtract_fusion
  230.2 1.5 fusion.19
  231.7 0.6 convert_reduce_fusion
  232.3 247.7 %psum.15 = f32[]{:T(128)} all-reduce(f32[]{:T(128)} %convert_reduce_fusion), channel_id=1, replica_groups=mesh['fsdp'=128,'tensor'=4] {'fsdp'}, use_global_device_ids=true, to_apply=%region_5.0 | all-reduce | flops 1 | bytes 8 | tf_op jit(solution)/shard_map/psum | solution.py:47
  480.0 0.5 broadcast.106
  480.5 0.7 reduce.8
  481.4 2.9 gather_fusion
  484.5 0.7 slice.10
  485.3 0.3 fusion.2
  497.2 5.0 copy.315
  502.3 1.2 reshape.203
  503.5 13.1 %all-to-all-start = ((bf16[128,2,200]{2,1,0:T(2,128)(2,1)}), bf16[128,2,200]{2,1,0:T(2,128)(2,1)S(1)}, u32[]{:S(2)}, u32[]{:S(2)}) async-start(bf16[128,2,200]{2,1,0:T(2,128)(2,1)} %reshape.203), calls=%async_computation | async-start | bytes 262144 | tf_op jit(solution)/shard_map/all_to_all | solution.py:65
  516.6 0.6 divide_add_fusion
  517.2 11.6 %all-to-all-done = bf16[128,2,200]{2,1,0:T(2,128)(2,1)S(1)} async-done(((bf16[128,2,200]{2,1,0:T(2,128)(2,1)}), bf16[128,2,200]{2,1,0:T(2,128)(2,1)S(1)}, u32[]{:S(2)}, u32[]{:S(2)}) %all-to-all-start) | async-done | bytes 102432 | tf_op jit(solution)/shard_map/all_to_all | solution.py:65
  528.8 0.6 reshape.204
  529.5 0.5 bitcast_bitcast_fusion
  530.0 1.3 reshape_reshape.3
  531.4 2.1 convolution_convert_fusion
  533.5 1.1 copy.327
  534.6 1.6 reshape.205
  536.2 10.1 %all-to-all-start.1 = ((bf16[128,2,200]{2,1,0:T(2,128)(2,1)}), bf16[128,2,200]{2,1,0:T(2,128)(2,1)S(1)}, u32[]{:S(2)}, u32[]{:S(2)}) async-start(bf16[128,2,200]{2,1,0:T(2,128)(2,1)} %reshape.205), calls=%async_computation.1 | async-start | bytes 262144 | tf_op jit(solution)/shard_map/all_to_all | solution.py:73
  546.3 1.0 divide_convert_fusion
  547.2 11.3 %all-to-all-done.1 = bf16[128,2,200]{2,1,0:T(2,128)(2,1)S(1)} async-done(((bf16[128,2,200]{2,1,0:T(2,128)(2,1)}), bf16[128,2,200]{2,1,0:T(2,128)(2,1)S(1)}, u32[]{:S(2)}, u32[]{:S(2)}) %all-to-all-start.1) | async-done | bytes 102432 | tf_op jit(solution)/shard_map/all_to_all | solution.py:73
  558.5 1.0 reshape.206
  559.5 2.3 copy.328
  561.8 0.7 copy.321
  562.5 1.1 copy.322
  (157 shorter events, 13.1 us)
Async XLA Ops:
  7.2 214.8 %all-reduce.2.cloned.1.call-start = ((), (), s32[]{:S(2)}) async-start(), calls=%async_computation.2 | async-start | bytes 3932160 | tf_op jit(solution)/shard_map/psum | solution.py:47
  14.6 0.7 copy-start.3
  14.6 466.8 %all-gather.6.cloned.1.call-start = ((), (), s32[]{:S(2)}) async-start(), calls=%async_computation.4 | async-start | bytes 4227072 | tf_op jit(solution)/shard_map/all_gather | solution.py:52
  227.6 4.1 copy-start.2
  227.6 253.7 %copy-start.1 = (bf16[2,20,1280]{2,0,1:T(2,128)(2,1)S(1)}, bf16[2,20,1280]{2,0,1:T(2,128)(2,1)}, u32[]{:S(2)}) copy-start(bf16[2,20,1280]{2,0,1:T(2,128)(2,1)} %param.8) | copy-start | bytes 307204
  231.7 299.7 %all-gather.4.cloned.1.call-start = ((), (), s32[]{:S(2)}) async-start(), calls=%async_computation.3 | async-start | bytes 1638400 | tf_op jit(solution)/shard_map/all_gather | solution.py:57
  503.5 25.4 %all-to-all-start = ((bf16[128,2,200]{2,1,0:T(2,128)(2,1)}), bf16[128,2,200]{2,1,0:T(2,128)(2,1)S(1)}, u32[]{:S(2)}, u32[]{:S(2)}) async-start(bf16[128,2,200]{2,1,0:T(2,128)(2,1)} %reshape.203), calls=%async_computation | async-start | bytes 262144 | tf_op jit(solution)/shard_map/all_to_all | solution.py:65
  533.5 12.8 %copy-start = (bf16[392,640]{1,0:T(8,128)(2,1)S(1)}, bf16[392,640]{1,0:T(8,128)(2,1)}, u32[]{:S(2)}) copy-start(bf16[392,640]{1,0:T(8,128)(2,1)} %param.9) | copy-start | bytes 1505284
  536.2 22.3 %all-to-all-start.1 = ((bf16[128,2,200]{2,1,0:T(2,128)(2,1)}), bf16[128,2,200]{2,1,0:T(2,128)(2,1)S(1)}, u32[]{:S(2)}, u32[]{:S(2)}) async-start(bf16[128,2,200]{2,1,0:T(2,128)(2,1)} %reshape.205), calls=%async_computation.1 | async-start | bytes 262144 | tf_op jit(solution)/shard_map/all_to_all | solution.py:73
Sparse Core Ops, SparseCore 0:
  14.8 207.1 all-reduce.1
  231.8 82.5 all-gather.5
  496.7 29.1 all-gather.3

commit v2 on v0

--- a/solution.py
+++ b/solution.py
@@ -49,7 +49,9 @@
     mine_blocks = jnp.einsum("sk,kij->sij", one_hot, factors, precision=lax.Precision.HIGHEST)
     held_inv = newton_inverse(mine_blocks) * jnp.max(one_hot, axis=1)[:, None, None]
     owner_out = held_inv[None]
-    shared = lax.all_gather(held_inv.astype(jnp.bfloat16), "fsdp", axis=0, tiled=True)
+    own = held_inv.astype(jnp.bfloat16)
+    repeated = jnp.stack([own] * lax.axis_size("fsdp"))
+    shared = jnp.concatenate(lax.all_to_all(repeated, "fsdp", 0, 0), axis=0)
     low_inv = jnp.take(shared, own_table, axis=0)
     low_inv = low_inv.reshape(layers, a_count + g_count, BLK, BLK)
     a_low = low_inv[:, :a_count]

time: 628 us -> 660 us (1.051)
  starting transfers between devices: 16.4 us -> 30.9 us
  waiting for transfers between devices: 310 us -> 323 us
    all_to_all x0 -> x1, waiting for transfers between devices: none -> 94 us  [on_device(): shared = jnp.concatenate(lax.all_to_all(repeated, 'fsdp', 0, 0), axis=0)]
    all_gather x1 -> x0, waiting for transfers between devices: 81.3 us -> none  [on_device(): lax.all_gather(held_inv.astype(jnp.bfloat16), 'fsdp', axis=0, tiled=True)]
    all_to_all x0 -> x1, starting transfers between devices: none -> 11.1 us  [on_device(): shared = jnp.concatenate(lax.all_to_all(repeated, 'fsdp', 0, 0), axis=0)]
where the time goes in v2:
time: 660 us; the launch traced here: 659 us
  waiting for transfers between devices  323 us (49%)
  blocking collectives  248 us (38%)
  starting transfers between devices  30.9 us (5%)
  local copies, waits for them, and re-layouts  23.9 us (4%)
  between operations  15.1 us (2%)
  matrix products  10.3 us (2%)
  other arithmetic  7.5 us (1%)
    psum x1, blocking collectives, on_device(): summed, count_total = lax.psum((partials, count_part), 'fsdp')  248 us
    psum x1, waiting for transfers between devices, on_device(): summed, count_total = lax.psum((partials, count_part), 'fsdp')  206 us
    all_to_all x1, waiting for transfers between devices, on_device(): shared = jnp.concatenate(lax.all_to_all(repeated, 'fsdp', 0, 0), axis=0)  94 us
    all_to_all x1, starting transfers between devices, on_device(): lax.all_to_all(right_done, 'fsdp', split_axis=2, concat_axis=1, tiled=True)  13.5 us
  transfers between devices with their start and end apart: 5, of which 4 were waited for; matrix products, arithmetic and copies ran while one was open for 1% of the time, Pallas kernels for 0%

profile of v2, /device:TPU:1, one launch (start us, length us, event | category | flops | bytes accessed | tf_op | source)
XLA Modules:
  0.0 659.2 jit_solution(9022765847620277455)
XLA Ops:
  7.2 2.8 copy.41
  10.1 0.9 fusion.20
  11.0 1.6 copy.43
  12.6 0.5 fusion.21
  13.1 1.4 pad_maximum_fusion
  14.6 0.6 copy-done.3
  15.2 0.6 fusion.14
  15.8 206.1 %all-reduce.2.cloned.1.call-done = f32[2,15,128,128]{3,2,1,0:T(8,128)} async-done(((f32[2,15,128,128]{3,2,1,0:T(8,128)}), f32[2,15,128,128]{3,2,1,0:T(8,128)}) %all-reduce.2.cloned.1.call-update) | async-done | bytes 1966096 | tf_op jit(solution)/shard_map/psum | solution.py:47
  221.9 1.7 broadcast_multiply_fusion
  223.6 1.9 fusion
  225.6 0.6 reduce_max.18
  226.9 0.2 convolution_subtract_fusion.7
  227.3 0.2 convolution_subtract_fusion.6
  227.8 0.2 convolution_subtract_fusion.5
  228.0 0.2 fusion.23
  228.2 0.2 convolution_subtract_fusion.4
  228.6 0.2 convolution_subtract_fusion.3
  229.0 0.2 convolution_subtract_fusion.2
  229.5 0.2 convolution_subtract_fusion.1
  229.9 0.2 convolution_subtract_fusion
  230.1 1.5 fusion.19
  231.6 3.0 stack.2
  234.6 11.1 %all-to-all-start = ((bf16[128,1,128,128]{3,2,1,0:T(8,128)(2,1)}), bf16[128,1,128,128]{3,2,1,0:T(8,128)(2,1)}, u32[]{:S(2)}, u32[]{:S(2)}) async-start(bf16[128,1,128,128]{3,2,1,0:T(8,128)(2,1)} %stack.2), calls=%async_computation | async-start | bytes 8388608 | tf_op jit(solution)/shard_map/all_to_all | solution.py:54
  245.8 0.5 broadcast.108
  246.3 0.7 reduce.8
  247.1 94.0 %all-to-all-done = bf16[128,1,128,128]{3,2,1,0:T(8,128)(2,1)} async-done(((bf16[128,1,128,128]{3,2,1,0:T(8,128)(2,1)}), bf16[128,1,128,128]{3,2,1,0:T(8,128)(2,1)}, u32[]{:S(2)}, u32[]{:S(2)}) %all-to-all-start) | async-done | bytes 4194336 | tf_op jit(solution)/shard_map/all_to_all | solution.py:54
  341.1 2.9 gather_fusion
  344.2 0.7 slice.10
  345.0 0.6 convert_reduce_fusion
  345.6 248.4 %psum.15 = f32[]{:T(128)} all-reduce(f32[]{:T(128)} %convert_reduce_fusion), channel_id=1, replica_groups=mesh['fsdp'=128,'tensor'=4] {'fsdp'}, use_global_device_ids=true, to_apply=%region_5.0 | all-reduce | flops 1 | bytes 8 | tf_op jit(solution)/shard_map/psum | solution.py:47
  594.1 0.3 fusion.2
  594.4 0.5 copy.59
  594.9 1.2 reshape.210
  596.1 13.5 %all-to-all-start.1 = ((bf16[128,2,200]{2,1,0:T(2,128)(2,1)}), bf16[128,2,200]{2,1,0:T(2,128)(2,1)S(1)}, u32[]{:S(2)}, u32[]{:S(2)}) async-start(bf16[128,2,200]{2,1,0:T(2,128)(2,1)} %reshape.210), calls=%async_computation.1 | async-start | bytes 262144 | tf_op jit(solution)/shard_map/all_to_all | solution.py:66
  609.6 0.7 divide_add_fusion
  610.3 11.6 %all-to-all-done.1 = bf16[128,2,200]{2,1,0:T(2,128)(2,1)S(1)} async-done(((bf16[128,2,200]{2,1,0:T(2,128)(2,1)}), bf16[128,2,200]{2,1,0:T(2,128)(2,1)S(1)}, u32[]{:S(2)}, u32[]{:S(2)}) %all-to-all-start.1) | async-done | bytes 102432 | tf_op jit(solution)/shard_map/all_to_all | solution.py:66
  621.9 0.6 reshape.211
  622.6 1.4 reshape.190
  624.0 2.1 convolution_convert_fusion
  626.1 1.1 copy.60
  627.2 1.6 reshape.212
  628.8 6.1 all-to-all-start.2
  634.9 1.0 divide_convert_fusion
  635.9 11.4 %all-to-all-done.2 = bf16[128,2,200]{2,1,0:T(2,128)(2,1)S(1)} async-done(((bf16[128,2,200]{2,1,0:T(2,128)(2,1)}), bf16[128,2,200]{2,1,0:T(2,128)(2,1)S(1)}, u32[]{:S(2)}, u32[]{:S(2)}) %all-to-all-start.2) | async-done | bytes 102432 | tf_op jit(solution)/shard_map/all_to_all | solution.py:73
  647.3 1.0 reshape.213
  648.3 2.3 copy.61
  650.6 0.7 copy.53
  651.3 1.1 copy.54
  (26 shorter events, 1.9 us)
Async XLA Ops:
  7.2 214.7 %all-reduce.2.cloned.1.call-start = ((), (), s32[]{:S(2)}) async-start(), calls=%async_computation.3 | async-start | bytes 3932160 | tf_op jit(solution)/shard_map/psum | solution.py:47
  14.6 0.7 copy-start.3
  234.6 106.5 %all-to-all-start = ((bf16[128,1,128,128]{3,2,1,0:T(8,128)(2,1)}), bf16[128,1,128,128]{3,2,1,0:T(8,128)(2,1)}, u32[]{:S(2)}, u32[]{:S(2)}) async-start(bf16[128,1,128,128]{3,2,1,0:T(8,128)(2,1)} %stack.2), calls=%async_computation | async-start | bytes 8388608 | tf_op jit(solution)/shard_map/all_to_all | solution.py:54
  245.7 378.3 %all-gather.2.cloned.1.call-start = ((), (), s32[]{:S(2)}) async-start(), calls=%async_computation.4 | async-start | bytes 1638400 | tf_op jit(solution)/shard_map/all_gather | solution.py:59
  344.0 1.0 copy-start.2
  344.0 250.0 %copy-start.1 = (bf16[2,20,1280]{2,0,1:T(2,128)(2,1)S(1)}, bf16[2,20,1280]{2,0,1:T(2,128)(2,1)}, u32[]{:S(2)}) copy-start(bf16[2,20,1280]{2,0,1:T(2,128)(2,1)} %param.8) | copy-start | bytes 307204
  596.1 25.8 %all-to-all-start.1 = ((bf16[128,2,200]{2,1,0:T(2,128)(2,1)}), bf16[128,2,200]{2,1,0:T(2,128)(2,1)S(1)}, u32[]{:S(2)}, u32[]{:S(2)}) async-start(bf16[128,2,200]{2,1,0:T(2,128)(2,1)} %reshape.210), calls=%async_computation.1 | async-start | bytes 262144 | tf_op jit(solution)/shard_map/all_to_all | solution.py:66
  626.1 8.8 %copy-start = (bf16[392,640]{1,0:T(8,128)(2,1)S(1)}, bf16[392,640]{1,0:T(8,128)(2,1)}, u32[]{:S(2)}) copy-start(bf16[392,640]{1,0:T(8,128)(2,1)} %param.9) | copy-start | bytes 1505284
  628.8 18.5 %all-to-all-start.2 = ((bf16[128,2,200]{2,1,0:T(2,128)(2,1)}), bf16[128,2,200]{2,1,0:T(2,128)(2,1)S(1)}, u32[]{:S(2)}, u32[]{:S(2)}) async-start(bf16[128,2,200]{2,1,0:T(2,128)(2,1)} %reshape.212), calls=%async_computation.2 | async-start | bytes 262144 | tf_op jit(solution)/shard_map/all_to_all | solution.py:73
Sparse Core Ops, SparseCore 0:
  14.7 207.1 all-reduce.1
  345.1 32.3 all-gather.1
